TPU v7x, 32 devices: a whole 2x2x4 slice. The times are simulated.
32 devices in a mesh: groups: 2 (over y), section: 4 (over z), seq: 4 (over x, core).
Axes of the slice: x: 2, y: 2, z: 4, core: 2. Of those that a mesh axis runs over, the one named last changes fastest.
Arguments:
- incoming_states: bfloat16 [1536, 3072], P('groups', 'seq'), parts along dimension 0, may hold values from -6 to 6
- transit_states: bfloat16 [4, 512, 3072], P('section', 'groups', 'seq'), parts along dimension 1, may hold values from -6 to 6
- patch_sizes_list: int32 [8], P('groups'), parts along dimension 0, may hold values from 1 to 256, 768 in all
- outdated_lookups: bfloat16 [4, 16, 1536, 128], P('section', 'seq', 'groups'), parts along dimension 2, may hold values from -6 to 6
- outdated_contents: bfloat16 [4, 16, 1536, 128], P('section', 'seq', 'groups'), parts along dimension 2, may hold values from -6 to 6
- attention_projection: bfloat16 [4, 3072, 6144], P('section', None, 'seq'), may hold values from -0.109375 to 0.109375
- exit_projection: bfloat16 [4, 2048, 3072], P('section', None, 'seq'), may hold values from -0.125 to 0.125
- shift_and_scale: float32 [4, 2, 3072], P('section'), may hold values from -3 to 3
- branch_gates: float32 [4, 3072], P('section', 'seq'), may hold values from -4 to 4
Outputs:
- section_out: bfloat16 [4, 4, 512, 3072], P(None, 'section', 'groups', 'seq'), parts along dimension 2
There are 2 independent parts, one for each index of `groups`. A program takes and returns all parts, laid end to end along the dimension named above; an argument that names none is the same for every part. Nothing has to cross between parts.
Inputs may be any that keep to these rules, and one draw needn't show every extreme that they name: `patch_sizes_list`: the 4 counts sum to 768; the largest equals 256.
All inputs are finite; a program needn't handle non-finite values.
Results may differ from a plain program's by a relative error of at most 0.005.
Values may be sent and summed in bfloat16 or wider, within the bound.
No kernel may reach another device: no remote copies, remote signals or barrier semaphores. Data moves between devices by JAX's collectives and lax.ppermute only.
A program may use at most 128 MiB of HBM per device.

v0:
```python
import jax
import jax.numpy as jnp
from jax import lax
from jax.sharding import PartitionSpec as P

epsilon = 1e-06


def passed_along(value, axis, steps):
    count = lax.axis_size(axis)
    leading, last = (max(0, -steps), min(count, count - steps))
    return lax.ppermute(value, axis, [(source, source + steps) for source in range(leading, last)])


def layer_norm(values):
    row_mean = jnp.mean(values, axis=-1, keepdims=True)
    centred = values - row_mean
    spread = jnp.mean(centred * centred, axis=-1, keepdims=True)
    return centred * lax.rsqrt(spread + epsilon)


def rms_norm(values):
    return values * lax.rsqrt(jnp.mean(values * values, axis=-1, keepdims=True) + epsilon)


def pick_entry(vector, position):
    return jnp.sum(jnp.where(jnp.arange(vector.shape[0]) == position, vector, 0))


def run_block(
    full_rows,
    own_rows,
    live_rows,
    patch_start,
    key_cache,
    value_cache,
    qkv_weights,
    shift_scale,
    gating_here,
    project,
):
    biggest_patch_span = full_rows.shape[0]
    heads_here = key_cache.shape[0]
    head_dim = key_cache.shape[2]
    seq_len = key_cache.shape[1] - biggest_patch_span
    shaped = (
        layer_norm(full_rows.astype(jnp.float32)) * (1.0 + shift_scale[1]) + shift_scale[0]
    ).astype(jnp.bfloat16)
    mixed = jnp.dot(shaped, qkv_weights, preferred_element_type=jnp.float32).reshape(
        biggest_patch_span, heads_here, 3, head_dim
    )
    queries = rms_norm(mixed[:, :, 0]).astype(jnp.bfloat16)
    fresh_keys = jnp.transpose(rms_norm(mixed[:, :, 1]).astype(jnp.bfloat16), (1, 0, 2))
    fresh_values = jnp.transpose(mixed[:, :, 2].astype(jnp.bfloat16), (1, 0, 2))
    mask = live_rows[None, :, None]
    window = lax.dynamic_slice_in_dim(key_cache, patch_start, biggest_patch_span, 1)
    key_cache = lax.dynamic_update_slice_in_dim(
        key_cache, jnp.where(mask, fresh_keys, window), patch_start, 1
    )
    window = lax.dynamic_slice_in_dim(value_cache, patch_start, biggest_patch_span, 1)
    value_cache = lax.dynamic_update_slice_in_dim(
        value_cache, jnp.where(mask, fresh_values, window), patch_start, 1
    )
    scores = jnp.einsum(
        "qhd,hkd->hqk", queries, key_cache[:, :seq_len], preferred_element_type=jnp.float32
    ) * head_dim ** (-0.5)
    expos = jnp.exp(scores)
    weights = (expos / jnp.sum(expos, axis=-1, keepdims=True)).astype(jnp.bfloat16)
    attended = jnp.einsum(
        "hqk,hkd->qhd", weights, value_cache[:, :seq_len], preferred_element_type=jnp.float32
    ).astype(jnp.bfloat16)
    head_rows = attended.reshape(biggest_patch_span, heads_here * head_dim)
    projected = project(head_rows)
    updated = own_rows.astype(jnp.float32) + gating_here * projected
    updated = jnp.where(live_rows[:, None], updated, 0.0).astype(jnp.bfloat16)
    return (updated, key_cache, value_cache)


def shards(
    incoming_states,
    transit_states,
    patch_sizes_list,
    outdated_lookups,
    outdated_contents,
    attention_projection,
    exit_projection,
    shift_and_scale,
    branch_gates,
):
    section_index = lax.axis_index("section")
    patches = patch_sizes_list.shape[0]
    biggest_patch_span = transit_states.shape[1]
    columns = incoming_states.shape[1]
    heads_here = outdated_lookups.shape[1]
    head_dim = outdated_lookups.shape[3]
    starts = jnp.cumsum(patch_sizes_list) - patch_sizes_list
    padding = jnp.zeros((heads_here, biggest_patch_span, head_dim), jnp.bfloat16)
    key_cache = jnp.concatenate([outdated_lookups[0], padding], axis=1)
    value_cache = jnp.concatenate([outdated_contents[0], padding], axis=1)
    qkv_weights = attention_projection[0]
    out_weights = exit_projection[0]
    shift_scale = shift_and_scale[0]
    gating_here = branch_gates[0]
    row_numbers = jnp.arange(biggest_patch_span)

    def gather_heads(head_rows):
        every_head = lax.all_gather(head_rows, "seq", axis=1, tiled=True)
        return jnp.dot(every_head, out_weights, preferred_element_type=jnp.float32)

    results = []
    entering_ext = jnp.concatenate(
        [incoming_states, jnp.zeros((biggest_patch_span, columns), jnp.bfloat16)], axis=0
    )
    earlier_result = transit_states[0]
    for turn_number in range(patches):
        patch_index = jnp.remainder(turn_number - section_index, patches)
        patch_count = pick_entry(patch_sizes_list, patch_index)
        patch_start = pick_entry(starts, patch_index)
        live_rows = row_numbers < patch_count
        entry_patch = lax.dynamic_slice_in_dim(
            entering_ext, starts[turn_number], biggest_patch_span, 0
        )
        own_rows = jnp.where(section_index == 0, entry_patch, earlier_result)
        own_rows = jnp.where(live_rows[:, None], own_rows, jnp.zeros_like(own_rows))
        full_rows = lax.all_gather(own_rows, "seq", axis=1, tiled=True)
        updated, key_cache, value_cache = run_block(
            full_rows,
            own_rows,
            live_rows,
            patch_start,
            key_cache,
            value_cache,
            qkv_weights,
            shift_scale,
            gating_here,
            gather_heads,
        )
        results.append(updated)
        if turn_number + 1 < patches:
            earlier_result = passed_along(updated, "section", 1)
    return jnp.stack(results)[:, None]


def solution(mesh):
    return jax.shard_map(
        shards,
        mesh=mesh,
        in_specs=(
            P("groups", "seq"),
            P("section", "groups", "seq"),
            P("groups"),
            P("section", "seq", "groups", None),
            P("section", "seq", "groups", None),
            P("section", None, "seq"),
            P("section", None, "seq"),
            P("section", None, None),
            P("section", "seq"),
        ),
        out_specs=P(None, "section", "groups", "seq"),
        check_vma=False,
    )
```

profile of v0, /device:TPU:0, one launch (start us, length us, event | category | flops | bytes accessed | tf_op | source)
XLA Modules:
  0.0 327.7 jit_solution(2446914256059857910)
XLA Ops:
  6.5 1.0 reduce-window.9
  7.5 1.5 fusion.146
  12.3 2.1 fusion.107
  15.7 2.3 copy.35
  18.1 2.3 copy.32
  20.4 2.3 concatenate.10
  22.6 2.3 concatenate.11
  24.9 12.7 %copy.33 = bf16[1,3072,1536]{1,2,0:T(8,128)(2,1)} copy(bf16[1,3072,1536]{2,1,0:T(8,128)(2,1)} %param.14) | data formatting | bytes 18874368 | tf_op args[5]
  38.3 1.8 convert_reduce_fusion.3
  40.2 2.0 fusion.20
  42.2 5.7 %fusion.37 = f32[256,4,3,128]{0,3,2,1:T(8,128)S(1)} fusion(bf16[4,3,128,3072]{3,2,1,0:T(8,128)(2,1)} %bitcast.213, bf16[256,3072]{1,0:T(8,128)(2,1)S(1)} %copy-done.3, f32[3072]{0:T(1024)S(1)} %bitcast.229, f32[3072]{0:T(1024)S(1)} %bitcast.225, f32[256]{0:T(256)S(1)} %add_rsqrt_fusion.11, f32[256]{0:T(256)S(1)} %broadcast_multiply_fusion.3), kind=kOutput, calls=%fused_computation.57 | convolution fusion | flops 2420637696 | bytes 12609536 | tf_op jit(solution)/shard_map/dot_general | solution.py:49
  48.0 1.1 fusion.129
  49.1 3.5 %dynamic_update_slice.24 = bf16[4,1024,128]{1,2,0:T(8,128)(2,1)} dynamic-update-slice(bf16[4,1024,128]{1,2,0:T(8,128)(2,1)} %concatenate.10, bf16[4,256,128]{1,2,0:T(8,128)(2,1)} %get-tuple-element.28, s32[]{:T(128)} %constant.58.clone.1, s32[]{:T(128)S(6)} %select_n.158, s32[]{:T(128)} %constant.58.clone.1) | dynamic-update-slice | bytes 524292 | tf_op jit(solution)/shard_map/dynamic_update_slice | solution.py:61
  52.6 3.4 %dynamic_update_slice.25 = bf16[4,1024,128]{1,2,0:T(8,128)(2,1)} dynamic-update-slice(bf16[4,1024,128]{1,2,0:T(8,128)(2,1)} %concatenate.11, bf16[4,256,128]{1,2,0:T(8,128)(2,1)S(1)} %get-tuple-element.29, s32[]{:T(128)} %constant.58.clone.1, s32[]{:T(128)S(6)} %select_n.158, s32[]{:T(128)} %constant.58.clone.1) | dynamic-update-slice | bytes 524292 | tf_op jit(solution)/shard_map/dynamic_update_slice | solution.py:57
  56.0 2.2 fusion.32
  58.2 1.5 fusion.92
  60.5 19.7 %all-gather.11.cloned.1.call-done = bf16[256,2048]{0,1:T(8,128)(2,1)} async-done(((bf16[256,512]{0,1:T(8,128)(2,1)}), bf16[256,2048]{0,1:T(8,128)(2,1)}) %all-gather.11.cloned.1.call-update) | async-done | bytes 1048592 | tf_op jit(solution)/shard_map/all_gather | solution.py:107
  80.2 3.0 fusion.86
  83.3 3.4 %collective-permute-start = (bf16[256,768]{1,0:T(8,128)(2,1)}, bf16[256,768]{1,0:T(8,128)(2,1)S(1)}, u32[]{:S(2)}, u32[]{:S(2)}) collective-permute-start(bf16[256,768]{1,0:T(8,128)(2,1)} %fusion.86), channel_id=1, source_target_pairs={{0,4},{4,8},{8,12},{1,5},{5,9},{9,13},{2,6},{6,10},{10,14},{3,7},{... | collective-permute-start | bytes 1179656 | tf_op jit(solution)/shard_map/ppermute | solution.py:12
  89.4 6.4 %collective-permute-done = bf16[256,768]{1,0:T(8,128)(2,1)S(1)} collective-permute-done((bf16[256,768]{1,0:T(8,128)(2,1)}, bf16[256,768]{1,0:T(8,128)(2,1)S(1)}, u32[]{:S(2)}, u32[]{:S(2)}) %collective-permute-start) | collective-permute-done | bytes 393248 | tf_op jit(solution)/shard_map/ppermute | solution.py:12
  95.7 2.0 fusion.109
  99.8 18.7 %all-gather.13.cloned.1.call-done = bf16[256,3072]{1,0:T(8,128)(2,1)} async-done(((bf16[256,768]{1,0:T(8,128)(2,1)}), bf16[256,3072]{1,0:T(8,128)(2,1)}) %all-gather.13.cloned.1.call-update) | async-done | bytes 1572880 | tf_op jit(solution)/shard_map/all_gather | solution.py:125
  118.4 1.8 convert_reduce_fusion.2
  120.3 2.0 fusion.16
  122.3 5.6 %fusion.40 = f32[256,4,3,128]{0,3,2,1:T(8,128)S(1)} fusion(bf16[4,3,128,3072]{3,2,1,0:T(8,128)(2,1)} %bitcast.214, bf16[256,3072]{1,0:T(8,128)(2,1)S(1)} %copy-done.5, f32[256]{0:T(256)S(1)} %add_rsqrt_fusion.10, f32[256]{0:T(256)S(1)} %broadcast_multiply_fusion.2, f32[3072]{0:T(1024)S(1)} %bitcast.230, f32[3072]{0:T(1024)S(1)} %bitcast.226), kind=kOutput, calls=%fused_computation.59 | convolution fusion | flops 2420637696 | bytes 12609536 | tf_op jit(solution)/shard_map/dot_general | solution.py:49
  128.0 1.0 copy-done.9
  129.0 2.1 fusion.131
  131.1 3.9 %dynamic_update_slice.26 = bf16[4,1024,128]{1,2,0:T(8,128)(2,1)} dynamic-update-slice(bf16[4,1024,128]{1,2,0:T(8,128)(2,1)} %dynamic_update_slice.24, bf16[4,256,128]{1,2,0:T(8,128)(2,1)} %get-tuple-element.26, s32[]{:T(128)} %constant.58.clone.1, s32[]{:T(128)S(6)} %select_n.168, s32[]{:T(128)} %constant.58.clone.1) | dynamic-update-slice | bytes 524292 | tf_op jit(solution)/shard_map/dynamic_update_slice | solution.py:61
  135.0 3.8 %dynamic_update_slice.27 = bf16[4,1024,128]{1,2,0:T(8,128)(2,1)} dynamic-update-slice(bf16[4,1024,128]{1,2,0:T(8,128)(2,1)} %dynamic_update_slice.25, bf16[4,256,128]{1,2,0:T(8,128)(2,1)S(1)} %get-tuple-element.27, s32[]{:T(128)} %constant.58.clone.1, s32[]{:T(128)S(6)} %select_n.168, s32[]{:T(128)} %constant.58.clone.1) | dynamic-update-slice | bytes 524292 | tf_op jit(solution)/shard_map/dynamic_update_slice | solution.py:57
  138.8 2.2 fusion.33
  141.0 1.5 fusion.91
  142.6 16.8 %all-gather.15.cloned.1.call-done = bf16[256,2048]{0,1:T(8,128)(2,1)} async-done(((bf16[256,512]{0,1:T(8,128)(2,1)}), bf16[256,2048]{0,1:T(8,128)(2,1)}) %all-gather.15.cloned.1.call-update) | async-done | bytes 1048592 | tf_op jit(solution)/shard_map/all_gather | solution.py:107
  159.5 3.0 select_convert_fusion.2
  162.5 3.4 %collective-permute-start.1 = (bf16[256,768]{1,0:T(8,128)(2,1)}, bf16[256,768]{1,0:T(8,128)(2,1)S(1)}, u32[]{:S(2)}, u32[]{:S(2)}) collective-permute-start(bf16[256,768]{1,0:T(8,128)(2,1)} %select_convert_fusion.2), channel_id=1, source_target_pairs={{0,4},{4,8},{8,12},{1,5},{5,9},{9,13},{2,6},{6,10},{10,14},{3,7},{... | collective-permute-start | bytes 1179656 | tf_op jit(solution)/shard_map/ppermute | solution.py:12
  168.6 6.3 %collective-permute-done.1 = bf16[256,768]{1,0:T(8,128)(2,1)S(1)} collective-permute-done((bf16[256,768]{1,0:T(8,128)(2,1)}, bf16[256,768]{1,0:T(8,128)(2,1)S(1)}, u32[]{:S(2)}, u32[]{:S(2)}) %collective-permute-start.1) | collective-permute-done | bytes 393248 | tf_op jit(solution)/shard_map/ppermute | solution.py:12
  174.9 2.0 fusion.111
  179.0 18.6 %all-gather.17.cloned.1.call-done = bf16[256,3072]{1,0:T(8,128)(2,1)} async-done(((bf16[256,768]{1,0:T(8,128)(2,1)}), bf16[256,3072]{1,0:T(8,128)(2,1)}) %all-gather.17.cloned.1.call-update) | async-done | bytes 1572880 | tf_op jit(solution)/shard_map/all_gather | solution.py:125
  197.6 1.8 convert_reduce_fusion.1
  199.4 2.0 fusion.12
  201.4 5.6 %fusion.43 = f32[256,4,3,128]{0,3,2,1:T(8,128)S(1)} fusion(bf16[4,3,128,3072]{3,2,1,0:T(8,128)(2,1)} %bitcast.215, bf16[256,3072]{1,0:T(8,128)(2,1)S(1)} %copy-done.6, f32[256]{0:T(256)S(1)} %add_rsqrt_fusion.9, f32[256]{0:T(256)S(1)} %broadcast_multiply_fusion.1, f32[3072]{0:T(1024)S(1)} %bitcast.231, f32[3072]{0:T(1024)S(1)} %bitcast.227), kind=kOutput, calls=%fused_computation.61 | convolution fusion | flops 2420637696 | bytes 12609536 | tf_op jit(solution)/shard_map/dot_general | solution.py:49
  207.2 1.0 copy-done.10
  208.2 2.1 fusion.133
  210.3 3.9 %dynamic_update_slice.28 = bf16[4,1024,128]{1,2,0:T(8,128)(2,1)} dynamic-update-slice(bf16[4,1024,128]{1,2,0:T(8,128)(2,1)} %dynamic_update_slice.26, bf16[4,256,128]{1,2,0:T(8,128)(2,1)} %get-tuple-element.24, s32[]{:T(128)} %constant.58.clone.1, s32[]{:T(128)S(6)} %select_n.178, s32[]{:T(128)} %constant.58.clone.1) | dynamic-update-slice | bytes 524292 | tf_op jit(solution)/shard_map/dynamic_update_slice | solution.py:61
  214.2 3.8 %dynamic_update_slice.29 = bf16[4,1024,128]{1,2,0:T(8,128)(2,1)} dynamic-update-slice(bf16[4,1024,128]{1,2,0:T(8,128)(2,1)} %dynamic_update_slice.27, bf16[4,256,128]{1,2,0:T(8,128)(2,1)S(1)} %get-tuple-element.25, s32[]{:T(128)} %constant.58.clone.1, s32[]{:T(128)S(6)} %select_n.178, s32[]{:T(128)} %constant.58.clone.1) | dynamic-update-slice | bytes 524292 | tf_op jit(solution)/shard_map/dynamic_update_slice | solution.py:57
  218.1 2.2 fusion.34
  220.2 1.5 fusion.90
  221.8 15.9 %all-gather.19.cloned.1.call-done = bf16[256,2048]{0,1:T(8,128)(2,1)} async-done(((bf16[256,512]{0,1:T(8,128)(2,1)}), bf16[256,2048]{0,1:T(8,128)(2,1)}) %all-gather.19.cloned.1.call-update) | async-done | bytes 1048592 | tf_op jit(solution)/shard_map/all_gather | solution.py:107
  237.7 3.0 select_convert_fusion.1
  240.7 3.6 %collective-permute-start.2 = (bf16[256,768]{1,0:T(8,128)(2,1)}, bf16[256,768]{1,0:T(8,128)(2,1)S(1)}, u32[]{:S(2)}, u32[]{:S(2)}) collective-permute-start(bf16[256,768]{1,0:T(8,128)(2,1)} %select_convert_fusion.1), channel_id=1, source_target_pairs={{0,4},{4,8},{8,12},{1,5},{5,9},{9,13},{2,6},{6,10},{10,14},{3,7},{... | collective-permute-start | bytes 1179656 | tf_op jit(solution)/shard_map/ppermute | solution.py:12
  246.8 6.3 %collective-permute-done.2 = bf16[256,768]{1,0:T(8,128)(2,1)S(1)} collective-permute-done((bf16[256,768]{1,0:T(8,128)(2,1)}, bf16[256,768]{1,0:T(8,128)(2,1)S(1)}, u32[]{:S(2)}, u32[]{:S(2)}) %collective-permute-start.2) | collective-permute-done | bytes 393248 | tf_op jit(solution)/shard_map/ppermute | solution.py:12
  253.2 1.9 fusion.113
  257.0 18.9 %all-gather.21.cloned.1.call-done = bf16[256,3072]{1,0:T(8,128)(2,1)} async-done(((bf16[256,768]{1,0:T(8,128)(2,1)}), bf16[256,3072]{1,0:T(8,128)(2,1)}) %all-gather.21.cloned.1.call-update) | async-done | bytes 1572880 | tf_op jit(solution)/shard_map/all_gather | solution.py:125
  275.9 1.8 convert_reduce_fusion
  277.7 2.0 fusion.8
  279.7 5.6 %fusion.46 = f32[256,4,3,128]{0,3,2,1:T(8,128)S(1)} fusion(bf16[4,3,128,3072]{3,2,1,0:T(8,128)(2,1)} %bitcast.216, bf16[256,3072]{1,0:T(8,128)(2,1)S(1)} %copy-done.4, f32[256]{0:T(256)S(1)} %add_rsqrt_fusion.8, f32[256]{0:T(256)S(1)} %broadcast_multiply_fusion, f32[3072]{0:T(1024)S(1)} %bitcast.232, f32[3072]{0:T(1024)S(1)} %bitcast.228), kind=kOutput, calls=%fused_computation.63 | convolution fusion | flops 2420637696 | bytes 12609536 | tf_op jit(solution)/shard_map/dot_general | solution.py:49
  285.4 1.0 copy-done.8
  286.4 2.1 fusion.135
  288.5 3.9 %dynamic_update_slice.30 = bf16[4,1024,128]{1,2,0:T(8,128)(2,1)} dynamic-update-slice(bf16[4,1024,128]{1,2,0:T(8,128)(2,1)} %dynamic_update_slice.28, bf16[4,256,128]{1,2,0:T(8,128)(2,1)} %get-tuple-element.18, s32[]{:T(128)} %constant.58.clone.1, s32[]{:T(128)S(6)} %select_n.188, s32[]{:T(128)} %constant.58.clone.1) | dynamic-update-slice | bytes 524292 | tf_op jit(solution)/shard_map/dynamic_update_slice | solution.py:61
  292.4 3.8 %dynamic_update_slice.31 = bf16[4,1024,128]{1,2,0:T(8,128)(2,1)} dynamic-update-slice(bf16[4,1024,128]{1,2,0:T(8,128)(2,1)} %dynamic_update_slice.29, bf16[4,256,128]{1,2,0:T(8,128)(2,1)S(1)} %get-tuple-element.19, s32[]{:T(128)} %constant.58.clone.1, s32[]{:T(128)S(6)} %select_n.188, s32[]{:T(128)} %constant.58.clone.1) | dynamic-update-slice | bytes 524292 | tf_op jit(solution)/shard_map/dynamic_update_slice | solution.py:57
  296.2 2.2 fusion.35
  298.4 1.5 fusion.89
  299.9 16.2 %all-gather.23.cloned.1.call-done = bf16[256,2048]{0,1:T(8,128)(2,1)} async-done(((bf16[256,512]{0,1:T(8,128)(2,1)}), bf16[256,2048]{0,1:T(8,128)(2,1)}) %all-gather.23.cloned.1.call-update) | async-done | bytes 1048592 | tf_op jit(solution)/shard_map/all_gather | solution.py:107
  316.0 2.2 fusion.105
  318.3 2.6 maximum_bitcast_fusion
  (107 shorter events, 5.1 us)
Async XLA Ops:
  6.5 73.7 %copy-start = (bf16[1,2048,768]{2,1,0:T(8,128)(2,1)S(1)}, bf16[1,2048,768]{2,1,0:T(8,128)(2,1)}, u32[]{:S(2)}) copy-start(bf16[1,2048,768]{2,1,0:T(8,128)(2,1)} %param.15) | copy-start | bytes 9437188
  6.5 31.8 %all-gather.9.cloned.1.call-start = ((), (), s32[]{:S(2)}) async-start(), calls=%async_computation | async-start | bytes 1966080 | tf_op jit(solution)/shard_map/all_gather | solution.py:125
  9.7 38.4 %copy-start.31 = (pred[256]{0:T(512)(128)(4,1)}, pred[256]{0:T(512)(128)(4,1)S(1)}, u32[]{:S(2)}) copy-start(pred[256]{0:T(512)(128)(4,1)S(1)} %iota_compare_fusion.3) | copy-start | bytes 772
  14.4 65.8 %all-gather.11.cloned.1.call-start = ((), (), s32[]{:S(2)}) async-start(), calls=%async_computation.1 | async-start | bytes 1310720 | tf_op jit(solution)/shard_map/all_gather | solution.py:107
  24.9 13.4 %copy-start.19 = (f32[1,2,3072]{2,1,0:T(2,128)S(1)}, f32[1,2,3072]{2,1,0:T(2,128)}, u32[]{:S(2)}) copy-start(f32[1,2,3072]{2,1,0:T(2,128)} %param.16) | copy-start | bytes 73732
  38.3 9.6 %copy-start.20 = (f32[1,1,3072]{2,1,0:T(1,128)}, f32[1,1,3072]{2,1,0:T(1,128)S(1)}, u32[]{:S(2)}) copy-start(f32[1,1,3072]{2,1,0:T(1,128)S(1)} %get-tuple-element.17) | copy-start | bytes 36868
  38.3 3.8 %copy-start.3 = (bf16[256,3072]{1,0:T(8,128)(2,1)S(1)}, bf16[256,3072]{1,0:T(8,128)(2,1)}, u32[]{:S(2)}) copy-start(bf16[256,3072]{1,0:T(8,128)(2,1)} %all-gather.9.cloned.1.call-done) | copy-start | bytes 4718596
  42.2 5.9 %copy-start.1 = (bf16[1,4,768,128]{2,3,1,0:T(8,128)(2,1)S(1)}, bf16[1,4,768,128]{2,3,1,0:T(8,128)(2,1)}, u32[]{:S(2)}) copy-start(bf16[1,4,768,128]{2,3,1,0:T(8,128)(2,1)} %copy.35) | copy-start | bytes 2359300
  42.2 5.9 %copy-start.2 = (bf16[1,4,768,128]{2,3,1,0:T(8,128)(2,1)S(1)}, bf16[1,4,768,128]{2,3,1,0:T(8,128)(2,1)}, u32[]{:S(2)}) copy-start(bf16[1,4,768,128]{2,3,1,0:T(8,128)(2,1)} %copy.32) | copy-start | bytes 2359300
  47.9 1.2 copy-start.7
  56.0 2.2 copy-start.11
  58.2 22.1 %copy-start.15 = (bf16[256,768]{1,0:T(8,128)(2,1)S(1)}, bf16[256,768]{1,0:T(8,128)(2,1)}, u32[]{:S(2)}) copy-start(bf16[256,768]{1,0:T(8,128)(2,1)} %fusion.107) | copy-start | bytes 1179652
  59.7 58.7 %all-gather.13.cloned.1.call-start = ((), (), s32[]{:S(2)}) async-start(), calls=%async_computation.2 | async-start | bytes 1966080 | tf_op jit(solution)/shard_map/all_gather | solution.py:125
  83.3 12.5 %collective-permute-start = (bf16[256,768]{1,0:T(8,128)(2,1)}, bf16[256,768]{1,0:T(8,128)(2,1)S(1)}, u32[]{:S(2)}, u32[]{:S(2)}) collective-permute-start(bf16[256,768]{1,0:T(8,128)(2,1)} %fusion.86), channel_id=1, source_target_pairs={{0,4},{4,8},{8,12},{1,5},{5,9},{9,13},{2,6},{6,10},{10,14},{3,7},{... | collective-permute-start | bytes 1179656 | tf_op jit(solution)/shard_map/ppermute | solution.py:12
  89.4 6.4 %copy-start.27 = (pred[256]{0:T(512)(128)(4,1)}, pred[256]{0:T(512)(128)(4,1)S(1)}, u32[]{:S(2)}) copy-start(pred[256]{0:T(512)(128)(4,1)S(1)} %iota_compare_fusion.2) | copy-start | bytes 772
  97.7 24.5 %copy-start.21 = (f32[1,1,3072]{2,1,0:T(1,128)S(1)}, f32[1,1,3072]{2,1,0:T(1,128)}, u32[]{:S(2)}) copy-start(f32[1,1,3072]{2,1,0:T(1,128)} %copy-done.20) | copy-start | bytes 36868
  97.7 61.7 %all-gather.15.cloned.1.call-start = ((), (), s32[]{:S(2)}) async-start(), calls=%async_computation.3 | async-start | bytes 1310720 | tf_op jit(solution)/shard_map/all_gather | solution.py:107
  118.4 3.8 %copy-start.5 = (bf16[256,3072]{1,0:T(8,128)(2,1)S(1)}, bf16[256,3072]{1,0:T(8,128)(2,1)}, u32[]{:S(2)}) copy-start(bf16[256,3072]{1,0:T(8,128)(2,1)} %all-gather.13.cloned.1.call-done) | copy-start | bytes 4718596
  122.2 6.7 %copy-start.28 = (pred[256]{0:T(512)(128)(4,1)S(1)}, pred[256]{0:T(512)(128)(4,1)}, u32[]{:S(2)}) copy-start(pred[256]{0:T(512)(128)(4,1)} %copy-done.27) | copy-start | bytes 772
  127.8 1.1 copy-start.9
  138.8 2.2 copy-start.12
  141.0 18.4 %copy-start.17 = (bf16[256,768]{1,0:T(8,128)(2,1)S(1)}, bf16[256,768]{1,0:T(8,128)(2,1)}, u32[]{:S(2)}) copy-start(bf16[256,768]{1,0:T(8,128)(2,1)} %fusion.109) | copy-start | bytes 1179652
  142.6 55.1 %all-gather.17.cloned.1.call-start = ((), (), s32[]{:S(2)}) async-start(), calls=%async_computation.4 | async-start | bytes 1966080 | tf_op jit(solution)/shard_map/all_gather | solution.py:125
  162.5 12.5 %collective-permute-start.1 = (bf16[256,768]{1,0:T(8,128)(2,1)}, bf16[256,768]{1,0:T(8,128)(2,1)S(1)}, u32[]{:S(2)}, u32[]{:S(2)}) collective-permute-start(bf16[256,768]{1,0:T(8,128)(2,1)} %select_convert_fusion.2), channel_id=1, source_target_pairs={{0,4},{4,8},{8,12},{1,5},{5,9},{9,13},{2,6},{6,10},{10,14},{3,7},{... | collective-permute-start | bytes 1179656 | tf_op jit(solution)/shard_map/ppermute | solution.py:12
  168.6 6.3 %copy-start.29 = (pred[256]{0:T(512)(128)(4,1)}, pred[256]{0:T(512)(128)(4,1)S(1)}, u32[]{:S(2)}) copy-start(pred[256]{0:T(512)(128)(4,1)S(1)} %iota_compare_fusion.1) | copy-start | bytes 772
  176.9 24.5 %copy-start.22 = (f32[1,1,3072]{2,1,0:T(1,128)S(1)}, f32[1,1,3072]{2,1,0:T(1,128)}, u32[]{:S(2)}) copy-start(f32[1,1,3072]{2,1,0:T(1,128)} %copy-done.20) | copy-start | bytes 36868
  176.9 60.8 %all-gather.19.cloned.1.call-start = ((), (), s32[]{:S(2)}) async-start(), calls=%async_computation.5 | async-start | bytes 1310720 | tf_op jit(solution)/shard_map/all_gather | solution.py:107
  197.6 3.8 %copy-start.6 = (bf16[256,3072]{1,0:T(8,128)(2,1)S(1)}, bf16[256,3072]{1,0:T(8,128)(2,1)}, u32[]{:S(2)}) copy-start(bf16[256,3072]{1,0:T(8,128)(2,1)} %all-gather.17.cloned.1.call-done) | copy-start | bytes 4718596
  201.4 6.7 %copy-start.30 = (pred[256]{0:T(512)(128)(4,1)S(1)}, pred[256]{0:T(512)(128)(4,1)}, u32[]{:S(2)}) copy-start(pred[256]{0:T(512)(128)(4,1)} %copy-done.29) | copy-start | bytes 772
  207.0 1.1 copy-start.10
  218.0 2.2 copy-start.13
  220.2 17.5 %copy-start.18 = (bf16[256,768]{1,0:T(8,128)(2,1)S(1)}, bf16[256,768]{1,0:T(8,128)(2,1)}, u32[]{:S(2)}) copy-start(bf16[256,768]{1,0:T(8,128)(2,1)} %fusion.111) | copy-start | bytes 1179652
  221.8 54.1 %all-gather.21.cloned.1.call-start = ((), (), s32[]{:S(2)}) async-start(), calls=%async_computation.6 | async-start | bytes 1966080 | tf_op jit(solution)/shard_map/all_gather | solution.py:125
  240.7 12.5 %collective-permute-start.2 = (bf16[256,768]{1,0:T(8,128)(2,1)}, bf16[256,768]{1,0:T(8,128)(2,1)S(1)}, u32[]{:S(2)}, u32[]{:S(2)}) collective-permute-start(bf16[256,768]{1,0:T(8,128)(2,1)} %select_convert_fusion.1), channel_id=1, source_target_pairs={{0,4},{4,8},{8,12},{1,5},{5,9},{9,13},{2,6},{6,10},{10,14},{3,7},{... | collective-permute-start | bytes 1179656 | tf_op jit(solution)/shard_map/ppermute | solution.py:12
  246.8 6.4 %copy-start.24 = (pred[256]{0:T(512)(128)(4,1)}, pred[256]{0:T(512)(128)(4,1)S(1)}, u32[]{:S(2)}) copy-start(pred[256]{0:T(512)(128)(4,1)S(1)} %iota_compare_fusion) | copy-start | bytes 772
  255.1 24.6 %copy-start.23 = (f32[1,1,3072]{2,1,0:T(1,128)S(1)}, f32[1,1,3072]{2,1,0:T(1,128)}, u32[]{:S(2)}) copy-start(f32[1,1,3072]{2,1,0:T(1,128)} %copy-done.20) | copy-start | bytes 36868
  255.1 61.0 %all-gather.23.cloned.1.call-start = ((), (), s32[]{:S(2)}) async-start(), calls=%async_computation.7 | async-start | bytes 1310720 | tf_op jit(solution)/shard_map/all_gather | solution.py:107
  275.9 3.8 %copy-start.4 = (bf16[256,3072]{1,0:T(8,128)(2,1)S(1)}, bf16[256,3072]{1,0:T(8,128)(2,1)}, u32[]{:S(2)}) copy-start(bf16[256,3072]{1,0:T(8,128)(2,1)} %all-gather.21.cloned.1.call-done) | copy-start | bytes 4718596
  279.7 6.7 %copy-start.25 = (pred[256]{0:T(512)(128)(4,1)S(1)}, pred[256]{0:T(512)(128)(4,1)}, u32[]{:S(2)}) copy-start(pred[256]{0:T(512)(128)(4,1)} %copy-done.24) | copy-start | bytes 772
  285.3 1.1 copy-start.8
  296.2 2.2 copy-start.14
  298.3 17.7 %copy-start.16 = (bf16[256,768]{1,0:T(8,128)(2,1)S(1)}, bf16[256,768]{1,0:T(8,128)(2,1)}, u32[]{:S(2)}) copy-start(bf16[256,768]{1,0:T(8,128)(2,1)} %fusion.113) | copy-start | bytes 1179652
  298.3 17.7 %copy-start.26 = (pred[256]{0:T(512)(128)(4,1)S(1)}, pred[256]{0:T(512)(128)(4,1)}, u32[]{:S(2)}) copy-start(pred[256]{0:T(512)(128)(4,1)} %copy-done.24) | copy-start | bytes 772
Sparse Core Ops, SparseCore 0:
  14.5 22.3 all-gather.8
  59.8 20.3 all-gather.10
  97.8 20.5 all-gather.12
  142.7 16.7 all-gather.14
  177.0 20.5 all-gather.16
  221.9 15.7 all-gather.18
  255.2 20.6 all-gather.20
  300.0 15.9 all-gather.22
where the time goes:
time: 330 us; the launch traced here: 328 us
  waiting for transfers between devices  144 us (44%)
  local copies, waits for them, and re-layouts  55.7 us (17%)
  matrix products  48.4 us (15%)
  other arithmetic  39.2 us (12%)
  between operations  29.6 us (9%)
  starting transfers between devices  10.9 us (3%)
    all_gather x4, waiting for transfers between devices, gather_heads(): every_head = lax.all_gather(head_rows, 'seq', axis=1, tiled=True)  68.6 us
    all_gather x4, waiting for transfers between devices, shards(): full_rows = lax.all_gather(own_rows, 'seq', axis=1, tiled=True)  56.1 us
    dot_general x4, matrix products, run_block(): jnp.dot(shaped, qkv_weights, preferred_element_type=jnp.float32)  22.4 us
    unnamed x67, local copies, waits for them, and re-layouts  20.5 us
    ppermute x3, waiting for transfers between devices, passed_along(): lax.ppermute(value, axis, [(source, source + steps) for source in range(l...  19 us
    dynamic_update_slice x4, local copies, waits for them, and re-layouts, run_block(): lax.dynamic_update_slice_in_dim(value_cache, jnp.where(mask, fresh_values...  15.2 us
    dynamic_update_slice x4, local copies, waits for them, and re-layouts, run_block(): lax.dynamic_update_slice_in_dim(key_cache, jnp.where(mask, fresh_keys, wi...  14.8 us
    dot_general x4, matrix products, gather_heads(): return jnp.dot(every_head, out_weights, preferred_element_type=jnp.float32)  11.3 us
  transfers between devices with their start and end apart: 11, of which 10 were waited for; matrix products, arithmetic and copies ran while one was open for 7% of the time, Pallas kernels for 0%

commit v1 on v0

--- a/solution.py
+++ b/solution.py
@@ -4,6 +4,22 @@
 from jax.sharding import PartitionSpec as P
 
 epsilon = 1e-06
+
+
+def gather_around(x, axis, dim):
+    ways, here, hop = (lax.axis_size(axis), lax.axis_index(axis), x.shape[dim])
+    dims = [n * ways if d == dim else n for d, n in enumerate(x.shape)]
+    full = lax.dynamic_update_slice_in_dim(jnp.zeros(dims, x.dtype), x, here * hop, axis=dim)
+    going_up = going_down = x
+    for far in range(1, ways // 2 + 1):
+        going_up = lax.ppermute(going_up, axis, [(d, (d + 1) % ways) for d in range(ways)])
+        full = lax.dynamic_update_slice_in_dim(full, going_up, (here - far) % ways * hop, axis=dim)
+        if 2 * far < ways:
+            going_down = lax.ppermute(going_down, axis, [(d, (d - 1) % ways) for d in range(ways)])
+            full = lax.dynamic_update_slice_in_dim(
+                full, going_down, (here + far) % ways * hop, axis=dim
+            )
+    return full
 
 
 def passed_along(value, axis, steps):
@@ -104,7 +120,7 @@
     row_numbers = jnp.arange(biggest_patch_span)
 
     def gather_heads(head_rows):
-        every_head = lax.all_gather(head_rows, "seq", axis=1, tiled=True)
+        every_head = gather_around(head_rows, "seq", 1)
         return jnp.dot(every_head, out_weights, preferred_element_type=jnp.float32)
 
     results = []

time: 330 us -> 309 us (0.936)
  waiting for transfers between devices: 144 us -> 112 us
  starting transfers between devices: 10.9 us -> 23.4 us
  matrix products: 48.4 us -> 43.5 us
  local copies, waits for them, and re-layouts: 55.7 us -> 59.5 us
    all_gather x4 -> x0, waiting for transfers between devices: 68.6 us -> none  [gather_heads(): every_head = lax.all_gather(head_rows, 'seq', axis=1, tiled=True)]
    ppermute x0 -> x12, waiting for transfers between devices: none -> 39.9 us  [the longest x8 39.9 us: gather_around(): lax.ppermute(going_up, axis, [(d, (d + 1) % ways) for d in range(ways)])]
    ppermute x0 -> x12, starting transfers between devices: none -> 10.3 us  [the longest x4 6.48 us: gather_around(): lax.ppermute(going_down, axis, [(d, (d - 1) % ways) for d in range(ways)])]
    ppermute x3, waiting for transfers between devices: 19 us -> 11.2 us  [passed_along(): lax.ppermute(value, axis, [(source, source + steps) for source in range(l...]
    dot_general x4, matrix products: 11.3 us -> 4.88 us  [gather_heads(): return jnp.dot(every_head, out_weights, preferred_element_type=jnp.float32)]
    all_gather x4, waiting for transfers between devices: 56.1 us -> 61.1 us  [shards(): full_rows = lax.all_gather(own_rows, 'seq', axis=1, tiled=True)]
    unnamed x67 -> x79, local copies, waits for them, and re-layouts: 20.5 us -> 20.6 us
  transfers between devices with their start and end apart: 11 -> 19, of which waited for: 10 -> 14; matrix products, arithmetic and copies ran while one was open for 7% -> 9% of each run, Pallas kernels for 0% -> 0%
where the time goes in v1:
time: 309 us; the launch traced here: 307 us
  waiting for transfers between devices  112 us (36%)
  local copies, waits for them, and re-layouts  59.5 us (19%)
  matrix products  43.5 us (14%)
  other arithmetic  38.8 us (13%)
  between operations  29.6 us (10%)
  starting transfers between devices  23.4 us (8%)
    all_gather x4, waiting for transfers between devices, shards(): full_rows = lax.all_gather(own_rows, 'seq', axis=1, tiled=True)  61.1 us
    ppermute x8, waiting for transfers between devices, gather_around(): lax.ppermute(going_up, axis, [(d, (d + 1) % ways) for d in range(ways)])  39.9 us
    dot_general x4, matrix products, run_block(): jnp.dot(shaped, qkv_weights, preferred_element_type=jnp.float32)  22.4 us
    unnamed x79, local copies, waits for them, and re-layouts  20.6 us
    dynamic_update_slice x4, local copies, waits for them, and re-layouts, run_block(): lax.dynamic_update_slice_in_dim(value_cache, jnp.where(mask, fresh_values...  15.1 us
    dynamic_update_slice x4, local copies, waits for them, and re-layouts, run_block(): lax.dynamic_update_slice_in_dim(key_cache, jnp.where(mask, fresh_keys, wi...  15 us
    ppermute x3, starting transfers between devices, passed_along(): lax.ppermute(value, axis, [(source, source + steps) for source in range(l...  12.7 us
    ppermute x3, waiting for transfers between devices, passed_along(): lax.ppermute(value, axis, [(source, source + steps) for source in range(l...  11.2 us
  transfers between devices with their start and end apart: 19, of which 14 were waited for; matrix products, arithmetic and copies ran while one was open for 9% of the time, Pallas kernels for 0%

profile of v1, /device:TPU:0, one launch (start us, length us, event | category | flops | bytes accessed | tf_op | source)
XLA Modules:
  0.0 307.0 jit_solution(11014535421936634107)
XLA Ops:
  7.5 1.5 fusion.169
  12.4 2.1 fusion.136
  15.8 12.7 %copy.33 = bf16[1,3072,1536]{1,2,0:T(8,128)(2,1)} copy(bf16[1,3072,1536]{2,1,0:T(8,128)(2,1)} %param.14) | data formatting | bytes 18874368 | tf_op args[5]
  28.6 2.3 copy.35
  30.9 2.3 copy.32
  33.9 2.3 concatenate.11
  36.1 2.3 concatenate.10
  38.5 1.8 convert_reduce_fusion.3
  40.3 2.0 fusion.20
  42.3 5.7 %fusion.37 = f32[256,4,3,128]{0,3,2,1:T(8,128)S(1)} fusion(bf16[4,3,128,3072]{3,2,1,0:T(8,128)(2,1)} %bitcast.227, bf16[256,3072]{1,0:T(8,128)(2,1)S(1)} %copy-done.3, f32[3072]{0:T(1024)S(1)} %bitcast.250, f32[3072]{0:T(1024)S(1)} %bitcast.246, f32[256]{0:T(256)S(1)} %add_rsqrt_fusion.11, f32[256]{0:T(256)S(1)} %broadcast_multiply_fusion.3), kind=kOutput, calls=%fused_computation.57 | convolution fusion | flops 2420637696 | bytes 12609536 | tf_op jit(solution)/shard_map/dot_general | solution.py:65
  48.2 1.1 fusion.152
  49.3 3.5 %dynamic_update_slice.73 = bf16[4,1024,128]{1,2,0:T(8,128)(2,1)} dynamic-update-slice(bf16[4,1024,128]{1,2,0:T(8,128)(2,1)} %concatenate.11, bf16[4,256,128]{1,2,0:T(8,128)(2,1)} %get-tuple-element.29, s32[]{:T(128)} %constant.95.clone.1, s32[]{:T(128)S(6)} %select_n.212, s32[]{:T(128)} %constant.95.clone.1) | dynamic-update-slice | bytes 524292 | tf_op jit(solution)/shard_map/dynamic_update_slice | solution.py:73
  52.7 3.6 %fusion.32 = (f32[4,256]{1,0:T(4,128)S(1)}, f32[4,256,768]{2,1,0:T(8,128)}) fusion(bf16[4,1024,128]{1,2,0:T(8,128)(2,1)} %dynamic_update_slice.73, f32[256,4,3,128]{0,3,2,1:T(8,128)} %copy-done.8, f32[256,4]{0,1:T(4,128)S(1)} %get-tuple-element.44), kind=kOutput, calls=%fused_computation.48 | convolution fusion | flops 203160576 | bytes 4464640 | tf_op jit(solution)/shard_map/qhd,hkd->hqk/dot_general | solution.py:80
  56.4 3.4 %dynamic_update_slice.72 = bf16[4,1024,128]{1,2,0:T(8,128)(2,1)} dynamic-update-slice(bf16[4,1024,128]{1,2,0:T(8,128)(2,1)} %concatenate.10, bf16[4,256,128]{1,2,0:T(8,128)(2,1)S(1)} %get-tuple-element.28, s32[]{:T(128)} %constant.95.clone.1, s32[]{:T(128)S(6)} %select_n.212, s32[]{:T(128)} %constant.95.clone.1) | dynamic-update-slice | bytes 524292 | tf_op jit(solution)/shard_map/dynamic_update_slice | solution.py:77
  59.8 3.6 %fusion.122 = bf16[4,128,256]{2,1,0:T(8,128)(2,1)} fusion(f32[4,256,768]{2,1,0:T(8,128)} %get-tuple-element.36, f32[4,256]{1,0:T(4,128)S(1)} %get-tuple-element.35, bf16[4,1024,128]{1,2,0:T(8,128)(2,1)} %dynamic_update_slice.72), kind=kOutput, calls=%fused_computation.105 | convolution fusion | flops 203816960 | bytes 4198400 | tf_op jit(solution)/shard_map/hqk,hkd->qhd/dot_general | solution.py:85
  63.8 2.0 collective-permute-start.1
  66.5 3.8 %collective-permute-done = bf16[256,512]{0,1:T(8,128)(2,1)} collective-permute-done((bf16[256,512]{0,1:T(8,128)(2,1)}, bf16[256,512]{0,1:T(8,128)(2,1)}, u32[]{:S(2)}, u32[]{:S(2)}) %collective-permute-start) | collective-permute-done | bytes 262176 | tf_op jit(solution)/shard_map/ppermute | solution.py:15
  70.3 2.6 collective-permute-start.2
  76.4 1.8 fusion.104
  78.1 5.9 %collective-permute-start.3 = (bf16[256,768]{1,0:T(8,128)(2,1)}, bf16[256,768]{1,0:T(8,128)(2,1)S(1)}, u32[]{:S(2)}, u32[]{:S(2)}) collective-permute-start(bf16[256,768]{1,0:T(8,128)(2,1)} %fusion.104), channel_id=1, source_target_pairs={{0,4},{4,8},{8,12},{1,5},{5,9},{9,13},{2,6},{6,10},{10,14},{3,7},{... | collective-permute-start | bytes 1179656 | tf_op jit(solution)/shard_map/ppermute | solution.py:28
  86.7 6.5 %collective-permute-done.3 = bf16[256,768]{1,0:T(8,128)(2,1)S(1)} collective-permute-done((bf16[256,768]{1,0:T(8,128)(2,1)}, bf16[256,768]{1,0:T(8,128)(2,1)S(1)}, u32[]{:S(2)}, u32[]{:S(2)}) %collective-permute-start.3) | collective-permute-done | bytes 393248 | tf_op jit(solution)/shard_map/ppermute | solution.py:28
  93.2 2.0 fusion.138
  97.2 19.0 %all-gather.7.cloned.1.call-done = bf16[256,3072]{1,0:T(8,128)(2,1)} async-done(((bf16[256,768]{1,0:T(8,128)(2,1)}), bf16[256,3072]{1,0:T(8,128)(2,1)}) %all-gather.7.cloned.1.call-update) | async-done | bytes 1572880 | tf_op jit(solution)/shard_map/all_gather | solution.py:141
  116.2 1.8 convert_reduce_fusion.2
  118.0 2.0 fusion.16
  120.0 5.6 %fusion.40 = f32[256,4,3,128]{0,3,2,1:T(8,128)S(1)} fusion(bf16[4,3,128,3072]{3,2,1,0:T(8,128)(2,1)} %bitcast.228, bf16[256,3072]{1,0:T(8,128)(2,1)S(1)} %copy-done.5, f32[256]{0:T(256)S(1)} %add_rsqrt_fusion.10, f32[256]{0:T(256)S(1)} %broadcast_multiply_fusion.2, f32[3072]{0:T(1024)S(1)} %bitcast.251, f32[3072]{0:T(1024)S(1)} %bitcast.247), kind=kOutput, calls=%fused_computation.59 | convolution fusion | flops 2420637696 | bytes 12609536 | tf_op jit(solution)/shard_map/dot_general | solution.py:65
  126.8 2.1 fusion.154
  128.8 3.9 %dynamic_update_slice.79 = bf16[4,1024,128]{1,2,0:T(8,128)(2,1)} dynamic-update-slice(bf16[4,1024,128]{1,2,0:T(8,128)(2,1)} %dynamic_update_slice.73, bf16[4,256,128]{1,2,0:T(8,128)(2,1)} %get-tuple-element.27, s32[]{:T(128)} %constant.95.clone.1, s32[]{:T(128)S(6)} %select_n.229, s32[]{:T(128)} %constant.95.clone.1) | dynamic-update-slice | bytes 524292 | tf_op jit(solution)/shard_map/dynamic_update_slice | solution.py:73
  132.8 3.9 %dynamic_update_slice.78 = bf16[4,1024,128]{1,2,0:T(8,128)(2,1)} dynamic-update-slice(bf16[4,1024,128]{1,2,0:T(8,128)(2,1)} %dynamic_update_slice.72, bf16[4,256,128]{1,2,0:T(8,128)(2,1)S(1)} %get-tuple-element.26, s32[]{:T(128)} %constant.95.clone.1, s32[]{:T(128)S(6)} %select_n.229, s32[]{:T(128)} %constant.95.clone.1) | dynamic-update-slice | bytes 524292 | tf_op jit(solution)/shard_map/dynamic_update_slice | solution.py:77
  136.6 2.2 fusion.33
  139.9 1.5 collective-permute-start.5
  141.4 6.3 %collective-permute-done.4 = bf16[256,512]{0,1:T(8,128)(2,1)S(1)} collective-permute-done((bf16[256,512]{0,1:T(8,128)(2,1)S(1)}, bf16[256,512]{0,1:T(8,128)(2,1)S(1)}, u32[]{:S(2)}, u32[]{:S(2)}) %collective-permute-start.4) | collective-permute-done | bytes 262176 | tf_op jit(solution)/shard_map/ppermute | solution.py:15
  147.9 5.6 %collective-permute-done.6 = bf16[256,512]{0,1:T(8,128)(2,1)S(1)} collective-permute-done((bf16[256,512]{0,1:T(8,128)(2,1)S(1)}, bf16[256,512]{0,1:T(8,128)(2,1)S(1)}, u32[]{:S(2)}, u32[]{:S(2)}) %collective-permute-start.6) | collective-permute-done | bytes 262176 | tf_op jit(solution)/shard_map/ppermute | solution.py:15
  153.6 1.0 fusion.107
  154.6 3.0 collective-permute-start.7
  160.3 2.2 collective-permute-done.7
  162.6 2.0 fusion.140
  166.6 21.8 %all-gather.9.cloned.1.call-done = bf16[256,3072]{1,0:T(8,128)(2,1)} async-done(((bf16[256,768]{1,0:T(8,128)(2,1)}), bf16[256,3072]{1,0:T(8,128)(2,1)}) %all-gather.9.cloned.1.call-update) | async-done | bytes 1572880 | tf_op jit(solution)/shard_map/all_gather | solution.py:141
  188.4 1.8 convert_reduce_fusion.1
  190.2 2.0 fusion.12
  192.2 5.6 %fusion.43 = f32[256,4,3,128]{0,3,2,1:T(8,128)S(1)} fusion(bf16[4,3,128,3072]{3,2,1,0:T(8,128)(2,1)} %bitcast.229, bf16[256,3072]{1,0:T(8,128)(2,1)S(1)} %copy-done.6, f32[256]{0:T(256)S(1)} %add_rsqrt_fusion.9, f32[256]{0:T(256)S(1)} %broadcast_multiply_fusion.1, f32[3072]{0:T(1024)S(1)} %bitcast.252, f32[3072]{0:T(1024)S(1)} %bitcast.248), kind=kOutput, calls=%fused_computation.61 | convolution fusion | flops 2420637696 | bytes 12609536 | tf_op jit(solution)/shard_map/dot_general | solution.py:65
  199.0 2.1 fusion.156
  201.1 3.9 %dynamic_update_slice.85 = bf16[4,1024,128]{1,2,0:T(8,128)(2,1)} dynamic-update-slice(bf16[4,1024,128]{1,2,0:T(8,128)(2,1)} %dynamic_update_slice.79, bf16[4,256,128]{1,2,0:T(8,128)(2,1)} %get-tuple-element.25, s32[]{:T(128)} %constant.95.clone.1, s32[]{:T(128)S(6)} %select_n.239, s32[]{:T(128)} %constant.95.clone.1) | dynamic-update-slice | bytes 524292 | tf_op jit(solution)/shard_map/dynamic_update_slice | solution.py:73
  205.0 3.9 %dynamic_update_slice.84 = bf16[4,1024,128]{1,2,0:T(8,128)(2,1)} dynamic-update-slice(bf16[4,1024,128]{1,2,0:T(8,128)(2,1)} %dynamic_update_slice.78, bf16[4,256,128]{1,2,0:T(8,128)(2,1)S(1)} %get-tuple-element.24, s32[]{:T(128)} %constant.95.clone.1, s32[]{:T(128)S(6)} %select_n.239, s32[]{:T(128)} %constant.95.clone.1) | dynamic-update-slice | bytes 524292 | tf_op jit(solution)/shard_map/dynamic_update_slice | solution.py:77
  208.9 2.2 fusion.34
  212.2 1.5 collective-permute-start.9
  213.7 6.3 %collective-permute-done.8 = bf16[256,512]{0,1:T(8,128)(2,1)S(1)} collective-permute-done((bf16[256,512]{0,1:T(8,128)(2,1)S(1)}, bf16[256,512]{0,1:T(8,128)(2,1)S(1)}, u32[]{:S(2)}, u32[]{:S(2)}) %collective-permute-start.8) | collective-permute-done | bytes 262176 | tf_op jit(solution)/shard_map/ppermute | solution.py:15
  220.2 5.6 %collective-permute-done.10 = bf16[256,512]{0,1:T(8,128)(2,1)S(1)} collective-permute-done((bf16[256,512]{0,1:T(8,128)(2,1)S(1)}, bf16[256,512]{0,1:T(8,128)(2,1)S(1)}, u32[]{:S(2)}, u32[]{:S(2)}) %collective-permute-start.10) | collective-permute-done | bytes 262176 | tf_op jit(solution)/shard_map/ppermute | solution.py:15
  225.8 1.0 fusion.110
  226.9 3.8 %collective-permute-start.11 = (bf16[256,768]{1,0:T(8,128)(2,1)S(1)}, bf16[256,768]{1,0:T(8,128)(2,1)}, u32[]{:S(2)}, u32[]{:S(2)}) collective-permute-start(bf16[256,768]{1,0:T(8,128)(2,1)S(1)} %fusion.110), channel_id=1, source_target_pairs={{0,4},{4,8},{8,12},{1,5},{5,9},{9,13},{2,6},{6,10},{10,14},{3,7},{... | collective-permute-start | bytes 1179656 | tf_op jit(solution)/shard_map/ppermute | solution.py:28
  233.2 2.5 collective-permute-done.11
  235.7 1.9 fusion.142
  239.5 20.3 %all-gather.11.cloned.1.call-done = bf16[256,3072]{1,0:T(8,128)(2,1)} async-done(((bf16[256,768]{1,0:T(8,128)(2,1)}), bf16[256,3072]{1,0:T(8,128)(2,1)}) %all-gather.11.cloned.1.call-update) | async-done | bytes 1572880 | tf_op jit(solution)/shard_map/all_gather | solution.py:141
  259.7 1.8 convert_reduce_fusion
  261.6 2.0 fusion.8
  263.6 5.6 %fusion.46 = f32[256,4,3,128]{0,3,2,1:T(8,128)S(1)} fusion(bf16[4,3,128,3072]{3,2,1,0:T(8,128)(2,1)} %bitcast.230, bf16[256,3072]{1,0:T(8,128)(2,1)S(1)} %copy-done.4, f32[256]{0:T(256)S(1)} %add_rsqrt_fusion.8, f32[256]{0:T(256)S(1)} %broadcast_multiply_fusion, f32[3072]{0:T(1024)S(1)} %bitcast.253, f32[3072]{0:T(1024)S(1)} %bitcast.249), kind=kOutput, calls=%fused_computation.63 | convolution fusion | flops 2420637696 | bytes 12609536 | tf_op jit(solution)/shard_map/dot_general | solution.py:65
  270.3 2.1 fusion.158
  272.4 3.9 %dynamic_update_slice.90 = bf16[4,1024,128]{1,2,0:T(8,128)(2,1)} dynamic-update-slice(bf16[4,1024,128]{1,2,0:T(8,128)(2,1)} %dynamic_update_slice.84, bf16[4,256,128]{1,2,0:T(8,128)(2,1)} %get-tuple-element.18, s32[]{:T(128)} %constant.95.clone.1, s32[]{:T(128)S(6)} %select_n.249, s32[]{:T(128)} %constant.95.clone.1) | dynamic-update-slice | bytes 524292 | tf_op jit(solution)/shard_map/dynamic_update_slice | solution.py:77
  276.3 3.8 %dynamic_update_slice.91 = bf16[4,1024,128]{1,2,0:T(8,128)(2,1)} dynamic-update-slice(bf16[4,1024,128]{1,2,0:T(8,128)(2,1)} %dynamic_update_slice.85, bf16[4,256,128]{1,2,0:T(8,128)(2,1)S(1)} %get-tuple-element.19, s32[]{:T(128)} %constant.95.clone.1, s32[]{:T(128)S(6)} %select_n.249, s32[]{:T(128)} %constant.95.clone.1) | dynamic-update-slice | bytes 524292 | tf_op jit(solution)/shard_map/dynamic_update_slice | solution.py:73
  280.0 2.2 fusion.35
  283.3 1.5 collective-permute-start.13
  284.8 6.3 %collective-permute-done.12 = bf16[256,512]{0,1:T(8,128)(2,1)S(1)} collective-permute-done((bf16[256,512]{0,1:T(8,128)(2,1)S(1)}, bf16[256,512]{0,1:T(8,128)(2,1)S(1)}, u32[]{:S(2)}, u32[]{:S(2)}) %collective-permute-start.12) | collective-permute-done | bytes 262176 | tf_op jit(solution)/shard_map/ppermute | solution.py:15
  291.3 5.6 %collective-permute-done.14 = bf16[256,512]{0,1:T(8,128)(2,1)S(1)} collective-permute-done((bf16[256,512]{0,1:T(8,128)(2,1)S(1)}, bf16[256,512]{0,1:T(8,128)(2,1)S(1)}, u32[]{:S(2)}, u32[]{:S(2)}) %collective-permute-start.14) | collective-permute-done | bytes 262176 | tf_op jit(solution)/shard_map/ppermute | solution.py:15
  298.1 2.3 maximum_bitcast_fusion
  (151 shorter events, 17.7 us)
Async XLA Ops:
  6.5 69.8 %copy-start = (bf16[1,2048,768]{2,1,0:T(8,128)(2,1)S(1)}, bf16[1,2048,768]{2,1,0:T(8,128)(2,1)}, u32[]{:S(2)}) copy-start(bf16[1,2048,768]{2,1,0:T(8,128)(2,1)} %param.15) | copy-start | bytes 9437188
  6.5 32.0 %all-gather.5.cloned.1.call-start = ((), (), s32[]{:S(2)}) async-start(), calls=%async_computation | async-start | bytes 1966080 | tf_op jit(solution)/shard_map/all_gather | solution.py:141
  11.7 36.5 %copy-start.36 = (pred[256]{0:T(512)(128)(4,1)}, pred[256]{0:T(512)(128)(4,1)S(1)}, u32[]{:S(2)}) copy-start(pred[256]{0:T(512)(128)(4,1)S(1)} %iota_compare_fusion.3) | copy-start | bytes 772
  14.5 101.7 %all-gather.7.cloned.1.call-start = ((), (), s32[]{:S(2)}) async-start(), calls=%async_computation.1 | async-start | bytes 1966080 | tf_op jit(solution)/shard_map/all_gather | solution.py:141
  28.6 9.8 %copy-start.22 = (f32[1,2,3072]{2,1,0:T(2,128)S(1)}, f32[1,2,3072]{2,1,0:T(2,128)}, u32[]{:S(2)}) copy-start(f32[1,2,3072]{2,1,0:T(2,128)} %param.16) | copy-start | bytes 73732
  38.5 9.6 %copy-start.23 = (f32[1,1,3072]{2,1,0:T(1,128)}, f32[1,1,3072]{2,1,0:T(1,128)S(1)}, u32[]{:S(2)}) copy-start(f32[1,1,3072]{2,1,0:T(1,128)S(1)} %get-tuple-element.17) | copy-start | bytes 36868
  38.5 3.8 %copy-start.3 = (bf16[256,3072]{1,0:T(8,128)(2,1)S(1)}, bf16[256,3072]{1,0:T(8,128)(2,1)}, u32[]{:S(2)}) copy-start(bf16[256,3072]{1,0:T(8,128)(2,1)} %all-gather.5.cloned.1.call-done) | copy-start | bytes 4718596
  42.3 5.9 %copy-start.1 = (bf16[1,4,768,128]{2,3,1,0:T(8,128)(2,1)S(1)}, bf16[1,4,768,128]{2,3,1,0:T(8,128)(2,1)}, u32[]{:S(2)}) copy-start(bf16[1,4,768,128]{2,3,1,0:T(8,128)(2,1)} %copy.35) | copy-start | bytes 2359300
  42.3 5.9 %copy-start.2 = (bf16[1,4,768,128]{2,3,1,0:T(8,128)(2,1)S(1)}, bf16[1,4,768,128]{2,3,1,0:T(8,128)(2,1)}, u32[]{:S(2)}) copy-start(bf16[1,4,768,128]{2,3,1,0:T(8,128)(2,1)} %copy.32) | copy-start | bytes 2359300
  48.1 1.2 copy-start.8
  63.4 12.9 %copy-start.14 = (bf16[256,768]{1,0:T(8,128)(2,1)S(1)}, bf16[256,768]{1,0:T(8,128)(2,1)}, u32[]{:S(2)}) copy-start(bf16[256,768]{1,0:T(8,128)(2,1)} %fusion.136) | copy-start | bytes 1179652
  63.4 6.9 %collective-permute-start = (bf16[256,512]{0,1:T(8,128)(2,1)}, bf16[256,512]{0,1:T(8,128)(2,1)}, u32[]{:S(2)}, u32[]{:S(2)}) collective-permute-start(bf16[256,512]{0,1:T(8,128)(2,1)} %bitcast.19), channel_id=1, source_target_pairs={{0,1},{1,2},{2,3},{3,0},{4,5},{5,6},{6,7},{7,4},{8,9},{9,10},{10,1... | collective-permute-start | bytes 786440 | tf_op jit(solution)/shard_map/ppermute | solution.py:15
  63.8 11.1 %collective-permute-start.1 = (bf16[256,512]{0,1:T(8,128)(2,1)}, bf16[256,512]{0,1:T(8,128)(2,1)}, u32[]{:S(2)}, u32[]{:S(2)}) collective-permute-start(bf16[256,512]{0,1:T(8,128)(2,1)} %bitcast.19), channel_id=1, source_target_pairs={{0,3},{1,0},{2,1},{3,2},{4,7},{5,4},{6,5},{7,6},{8,11},{9,8},{10,9... | collective-permute-start | bytes 786440 | tf_op jit(solution)/shard_map/ppermute | solution.py:18
  66.5 9.9 %copy-start.37 = (pred[256]{0:T(512)(128)(4,1)S(1)}, pred[256]{0:T(512)(128)(4,1)}, u32[]{:S(2)}) copy-start(pred[256]{0:T(512)(128)(4,1)} %copy-done.36) | copy-start | bytes 772
  70.3 6.0 %collective-permute-start.2 = (bf16[256,512]{0,1:T(8,128)(2,1)}, bf16[256,512]{0,1:T(8,128)(2,1)S(1)}, u32[]{:S(2)}, u32[]{:S(2)}) collective-permute-start(bf16[256,512]{0,1:T(8,128)(2,1)} %collective-permute-done), channel_id=1, source_target_pairs={{0,1},{1,2},{2,3},{3,0},{4,5},{5,6},{6,7},{7,4},{8,9},{9,10},{10,1... | collective-permute-start | bytes 786440 | tf_op jit(solution)/shard_map/ppermute | solution.py:15
  78.1 15.0 %collective-permute-start.3 = (bf16[256,768]{1,0:T(8,128)(2,1)}, bf16[256,768]{1,0:T(8,128)(2,1)S(1)}, u32[]{:S(2)}, u32[]{:S(2)}) collective-permute-start(bf16[256,768]{1,0:T(8,128)(2,1)} %fusion.104), channel_id=1, source_target_pairs={{0,4},{4,8},{8,12},{1,5},{5,9},{9,13},{2,6},{6,10},{10,14},{3,7},{... | collective-permute-start | bytes 1179656 | tf_op jit(solution)/shard_map/ppermute | solution.py:28
  86.7 6.5 %copy-start.30 = (pred[256]{0:T(512)(128)(4,1)}, pred[256]{0:T(512)(128)(4,1)S(1)}, u32[]{:S(2)}) copy-start(pred[256]{0:T(512)(128)(4,1)S(1)} %iota_compare_fusion.2) | copy-start | bytes 772
  95.1 24.9 %copy-start.24 = (f32[1,1,3072]{2,1,0:T(1,128)S(1)}, f32[1,1,3072]{2,1,0:T(1,128)}, u32[]{:S(2)}) copy-start(f32[1,1,3072]{2,1,0:T(1,128)} %copy-done.23) | copy-start | bytes 36868
  95.1 93.3 %all-gather.9.cloned.1.call-start = ((), (), s32[]{:S(2)}) async-start(), calls=%async_computation.2 | async-start | bytes 1966080 | tf_op jit(solution)/shard_map/all_gather | solution.py:141
  116.2 3.8 %copy-start.5 = (bf16[256,3072]{1,0:T(8,128)(2,1)S(1)}, bf16[256,3072]{1,0:T(8,128)(2,1)}, u32[]{:S(2)}) copy-start(bf16[256,3072]{1,0:T(8,128)(2,1)} %all-gather.7.cloned.1.call-done) | copy-start | bytes 4718596
  120.0 6.7 %copy-start.31 = (pred[256]{0:T(512)(128)(4,1)S(1)}, pred[256]{0:T(512)(128)(4,1)}, u32[]{:S(2)}) copy-start(pred[256]{0:T(512)(128)(4,1)} %copy-done.30) | copy-start | bytes 772
  125.6 1.1 copy-start.9
  136.6 2.2 copy-start.11
  139.6 13.9 %copy-start.16 = (bf16[256,768]{1,0:T(8,128)(2,1)S(1)}, bf16[256,768]{1,0:T(8,128)(2,1)}, u32[]{:S(2)}) copy-start(bf16[256,768]{1,0:T(8,128)(2,1)} %fusion.138) | copy-start | bytes 1179652
  139.6 13.9 %copy-start.32 = (pred[256]{0:T(512)(128)(4,1)S(1)}, pred[256]{0:T(512)(128)(4,1)}, u32[]{:S(2)}) copy-start(pred[256]{0:T(512)(128)(4,1)} %copy-done.30) | copy-start | bytes 772
  139.6 8.1 %collective-permute-start.4 = (bf16[256,512]{0,1:T(8,128)(2,1)S(1)}, bf16[256,512]{0,1:T(8,128)(2,1)S(1)}, u32[]{:S(2)}, u32[]{:S(2)}) collective-permute-start(bf16[256,512]{0,1:T(8,128)(2,1)S(1)} %bitcast.240), channel_id=1, source_target_pairs={{0,1},{1,2},{2,3},{3,0},{4,5},{5,6},{6,7},{7,4},{8,9},{9,10},{10,1... | collective-permute-start | bytes 786440 | tf_op jit(solution)/shard_map/ppermute | solution.py:15
  139.9 7.9 %collective-permute-start.5 = (bf16[256,512]{0,1:T(8,128)(2,1)S(1)}, bf16[256,512]{0,1:T(8,128)(2,1)S(1)}, u32[]{:S(2)}, u32[]{:S(2)}) collective-permute-start(bf16[256,512]{0,1:T(8,128)(2,1)S(1)} %bitcast.241), channel_id=1, source_target_pairs={{0,3},{1,0},{2,1},{3,2},{4,7},{5,4},{6,5},{7,6},{8,11},{9,8},{10,9... | collective-permute-start | bytes 786440 | tf_op jit(solution)/shard_map/ppermute | solution.py:18
  147.7 5.8 %collective-permute-start.6 = (bf16[256,512]{0,1:T(8,128)(2,1)S(1)}, bf16[256,512]{0,1:T(8,128)(2,1)S(1)}, u32[]{:S(2)}, u32[]{:S(2)}) collective-permute-start(bf16[256,512]{0,1:T(8,128)(2,1)S(1)} %collective-permute-done.4), channel_id=1, source_target_pairs={{0,1},{1,2},{2,3},{3,0},{4,5},{5,6},{6,7},{7,4},{8,9},{9,10},{10,1... | collective-permute-start | bytes 786440 | tf_op jit(solution)/shard_map/ppermute | solution.py:15
  154.6 43.2 %copy-start.18 = (bf16[256,768]{1,0:T(8,128)(2,1)}, bf16[256,768]{1,0:T(8,128)(2,1)S(1)}, u32[]{:S(2)}) copy-start(bf16[256,768]{1,0:T(8,128)(2,1)S(1)} %fusion.107) | copy-start | bytes 1179652
  154.6 7.9 %collective-permute-start.7 = (bf16[256,768]{1,0:T(8,128)(2,1)S(1)}, bf16[256,768]{1,0:T(8,128)(2,1)}, u32[]{:S(2)}, u32[]{:S(2)}) collective-permute-start(bf16[256,768]{1,0:T(8,128)(2,1)S(1)} %fusion.107), channel_id=1, source_target_pairs={{0,4},{4,8},{8,12},{1,5},{5,9},{9,13},{2,6},{6,10},{10,14},{3,7},{... | collective-permute-start | bytes 1179656 | tf_op jit(solution)/shard_map/ppermute | solution.py:28
  160.3 2.2 copy-start.33
  164.5 95.2 %all-gather.11.cloned.1.call-start = ((), (), s32[]{:S(2)}) async-start(), calls=%async_computation.3 | async-start | bytes 1966080 | tf_op jit(solution)/shard_map/all_gather | solution.py:141
  188.4 3.8 %copy-start.6 = (bf16[256,3072]{1,0:T(8,128)(2,1)S(1)}, bf16[256,3072]{1,0:T(8,128)(2,1)}, u32[]{:S(2)}) copy-start(bf16[256,3072]{1,0:T(8,128)(2,1)} %all-gather.9.cloned.1.call-done) | copy-start | bytes 4718596
  188.4 3.8 %copy-start.25 = (f32[1,1,3072]{2,1,0:T(1,128)S(1)}, f32[1,1,3072]{2,1,0:T(1,128)}, u32[]{:S(2)}) copy-start(f32[1,1,3072]{2,1,0:T(1,128)} %copy-done.23) | copy-start | bytes 36868
  192.2 6.8 %copy-start.34 = (pred[256]{0:T(512)(128)(4,1)S(1)}, pred[256]{0:T(512)(128)(4,1)}, u32[]{:S(2)}) copy-start(pred[256]{0:T(512)(128)(4,1)} %copy-done.33) | copy-start | bytes 772
  197.8 1.1 copy-start.10
  208.9 2.2 copy-start.12
  211.9 13.9 %copy-start.17 = (bf16[256,768]{1,0:T(8,128)(2,1)S(1)}, bf16[256,768]{1,0:T(8,128)(2,1)}, u32[]{:S(2)}) copy-start(bf16[256,768]{1,0:T(8,128)(2,1)} %fusion.140) | copy-start | bytes 1179652
  211.9 13.9 %copy-start.35 = (pred[256]{0:T(512)(128)(4,1)S(1)}, pred[256]{0:T(512)(128)(4,1)}, u32[]{:S(2)}) copy-start(pred[256]{0:T(512)(128)(4,1)} %copy-done.33) | copy-start | bytes 772
  211.9 8.1 %collective-permute-start.8 = (bf16[256,512]{0,1:T(8,128)(2,1)S(1)}, bf16[256,512]{0,1:T(8,128)(2,1)S(1)}, u32[]{:S(2)}, u32[]{:S(2)}) collective-permute-start(bf16[256,512]{0,1:T(8,128)(2,1)S(1)} %bitcast.243), channel_id=1, source_target_pairs={{0,1},{1,2},{2,3},{3,0},{4,5},{5,6},{6,7},{7,4},{8,9},{9,10},{10,1... | collective-permute-start | bytes 786440 | tf_op jit(solution)/shard_map/ppermute | solution.py:15
  212.2 7.9 %collective-permute-start.9 = (bf16[256,512]{0,1:T(8,128)(2,1)S(1)}, bf16[256,512]{0,1:T(8,128)(2,1)S(1)}, u32[]{:S(2)}, u32[]{:S(2)}) collective-permute-start(bf16[256,512]{0,1:T(8,128)(2,1)S(1)} %bitcast.244), channel_id=1, source_target_pairs={{0,3},{1,0},{2,1},{3,2},{4,7},{5,4},{6,5},{7,6},{8,11},{9,8},{10,9... | collective-permute-start | bytes 786440 | tf_op jit(solution)/shard_map/ppermute | solution.py:18
  220.0 5.8 %collective-permute-start.10 = (bf16[256,512]{0,1:T(8,128)(2,1)S(1)}, bf16[256,512]{0,1:T(8,128)(2,1)S(1)}, u32[]{:S(2)}, u32[]{:S(2)}) collective-permute-start(bf16[256,512]{0,1:T(8,128)(2,1)S(1)} %collective-permute-done.8), channel_id=1, source_target_pairs={{0,1},{1,2},{2,3},{3,0},{4,5},{5,6},{6,7},{7,4},{8,9},{9,10},{10,1... | collective-permute-start | bytes 786440 | tf_op jit(solution)/shard_map/ppermute | solution.py:15
  226.9 42.3 %copy-start.20 = (bf16[256,768]{1,0:T(8,128)(2,1)}, bf16[256,768]{1,0:T(8,128)(2,1)S(1)}, u32[]{:S(2)}) copy-start(bf16[256,768]{1,0:T(8,128)(2,1)S(1)} %fusion.110) | copy-start | bytes 1179652
  226.9 8.8 %collective-permute-start.11 = (bf16[256,768]{1,0:T(8,128)(2,1)S(1)}, bf16[256,768]{1,0:T(8,128)(2,1)}, u32[]{:S(2)}, u32[]{:S(2)}) collective-permute-start(bf16[256,768]{1,0:T(8,128)(2,1)S(1)} %fusion.110), channel_id=1, source_target_pairs={{0,4},{4,8},{8,12},{1,5},{5,9},{9,13},{2,6},{6,10},{10,14},{3,7},{... | collective-permute-start | bytes 1179656 | tf_op jit(solution)/shard_map/ppermute | solution.py:28
  233.2 2.5 copy-start.27
  259.7 3.8 %copy-start.4 = (bf16[256,3072]{1,0:T(8,128)(2,1)S(1)}, bf16[256,3072]{1,0:T(8,128)(2,1)}, u32[]{:S(2)}) copy-start(bf16[256,3072]{1,0:T(8,128)(2,1)} %all-gather.11.cloned.1.call-done) | copy-start | bytes 4718596
  259.7 3.8 %copy-start.26 = (f32[1,1,3072]{2,1,0:T(1,128)S(1)}, f32[1,1,3072]{2,1,0:T(1,128)}, u32[]{:S(2)}) copy-start(f32[1,1,3072]{2,1,0:T(1,128)} %copy-done.23) | copy-start | bytes 36868
  263.5 6.8 %copy-start.28 = (pred[256]{0:T(512)(128)(4,1)S(1)}, pred[256]{0:T(512)(128)(4,1)}, u32[]{:S(2)}) copy-start(pred[256]{0:T(512)(128)(4,1)} %copy-done.27) | copy-start | bytes 772
  269.2 1.1 copy-start.7
  280.0 2.2 copy-start.13
  283.0 13.9 %copy-start.15 = (bf16[256,768]{1,0:T(8,128)(2,1)S(1)}, bf16[256,768]{1,0:T(8,128)(2,1)}, u32[]{:S(2)}) copy-start(bf16[256,768]{1,0:T(8,128)(2,1)} %fusion.142) | copy-start | bytes 1179652
  283.0 13.9 %copy-start.29 = (pred[256]{0:T(512)(128)(4,1)S(1)}, pred[256]{0:T(512)(128)(4,1)}, u32[]{:S(2)}) copy-start(pred[256]{0:T(512)(128)(4,1)} %copy-done.27) | copy-start | bytes 772
  283.0 8.1 %collective-permute-start.12 = (bf16[256,512]{0,1:T(8,128)(2,1)S(1)}, bf16[256,512]{0,1:T(8,128)(2,1)S(1)}, u32[]{:S(2)}, u32[]{:S(2)}) collective-permute-start(bf16[256,512]{0,1:T(8,128)(2,1)S(1)} %bitcast.237), channel_id=1, source_target_pairs={{0,1},{1,2},{2,3},{3,0},{4,5},{5,6},{6,7},{7,4},{8,9},{9,10},{10,1... | collective-permute-start | bytes 786440 | tf_op jit(solution)/shard_map/ppermute | solution.py:15
  283.3 7.9 %collective-permute-start.13 = (bf16[256,512]{0,1:T(8,128)(2,1)S(1)}, bf16[256,512]{0,1:T(8,128)(2,1)S(1)}, u32[]{:S(2)}, u32[]{:S(2)}) collective-permute-start(bf16[256,512]{0,1:T(8,128)(2,1)S(1)} %bitcast.238), channel_id=1, source_target_pairs={{0,3},{1,0},{2,1},{3,2},{4,7},{5,4},{6,5},{7,6},{8,11},{9,8},{10,9... | collective-permute-start | bytes 786440 | tf_op jit(solution)/shard_map/ppermute | solution.py:18
  291.1 5.8 %collective-permute-start.14 = (bf16[256,512]{0,1:T(8,128)(2,1)S(1)}, bf16[256,512]{0,1:T(8,128)(2,1)S(1)}, u32[]{:S(2)}, u32[]{:S(2)}) collective-permute-start(bf16[256,512]{0,1:T(8,128)(2,1)S(1)} %collective-permute-done.12), channel_id=1, source_target_pairs={{0,1},{1,2},{2,3},{3,0},{4,5},{5,6},{6,7},{7,4},{8,9},{9,10},{10,1... | collective-permute-start | bytes 786440 | tf_op jit(solution)/shard_map/ppermute | solution.py:15
  297.0 1.1 copy-start.19
  297.0 1.1 copy-start.21
Sparse Core Ops, SparseCore 0:
  14.7 22.3 all-gather.4
  95.3 20.9 all-gather.6
  164.7 23.7 all-gather.8
  237.7 21.9 all-gather.10
